TPU v7x, 512 devices: a whole 4x4x16 slice. The times are simulated.
512 devices in a mesh: seq: 64 (over x, z), head: 8 (over y, core).
Axes of the slice: x: 4, y: 4, z: 16, core: 2. Of those that a mesh axis runs over, the one named last changes fastest.
Arguments:
- queries: bfloat16 [8192, 4096], P('seq', 'head'), may hold values from -6 to 6
- keys: bfloat16 [8192, 4096], P('seq', 'head'), may hold values from -6 to 6
- values: bfloat16 [8192, 4096], P('seq', 'head'), may hold values from -6 to 6
- log_decay: float32 [8192, 32], P('seq', 'head'), may hold values from -0.75 to 0
- norm_gain: float32 [4096], P('head'), may hold values from 0.1 to 1.9
- out_weight: bfloat16 [4096, 4096], P('head'), may hold values from -0.125 to 0.125
- steer_ids: int32 [8192], P('seq'), may hold values from 0 to 15
- steer_table: bfloat16 [16, 4096], P(None, 'head'), may hold values from -3 to 3
Outputs:
- layer_out: bfloat16 [8192, 4096], P('seq', 'head')
All inputs are finite; a program needn't handle non-finite values.
Results may differ from a plain program's by a relative error of at most 0.0052.
Values sent between devices are 32-bit elements; how exact they have to be, the bound alone decides.
No kernel may reach another device: no remote copies, remote signals or barrier semaphores. Data moves between devices by JAX's collectives and lax.ppermute only.
A program may use at most 64 MiB of HBM per device.

v0:
```python
import jax
import jax.numpy as jnp
from jax import lax
from jax.sharding import PartitionSpec as P

SPAN = 128


def prefix(part, axis, combine, identity):
    place = lax.axis_index(axis)
    gathered = jax.tree.map(lambda a: lax.all_gather(a, axis), part)
    state = jax.tree.map(lambda a, e: jnp.zeros_like(a) + jnp.asarray(e, a.dtype), part, identity)

    def one(step, state):
        return combine(
            state, jax.tree.map(lambda a: lax.dynamic_index_in_dim(a, step, 0, False), gathered)
        )

    return lax.fori_loop(0, place, one, state)


def block_step(state, inputs):
    query, key_blk, value_blk, decay = inputs
    cum = jnp.cumsum(decay, axis=1)
    size = decay.shape[1]
    rows = lax.broadcasted_iota(jnp.int32, (size, size), 0)
    cols = lax.broadcasted_iota(jnp.int32, (size, size), 1)
    lower = (cols <= rows)[None]
    scores = jnp.einsum("hte,hse->hts", query, key_blk, preferred_element_type=jnp.float32)
    diffs = jnp.where(lower, cum[:, :, None] - cum[:, None, :], 0.0)
    block_weights = (jnp.where(lower, jnp.exp(diffs), 0.0) * scores).astype(jnp.bfloat16)
    intra = jnp.einsum("hts,hse->hte", block_weights, value_blk, preferred_element_type=jnp.float32)
    inter = jnp.exp(cum)[:, :, None] * jnp.einsum(
        "hte,hef->htf", query.astype(jnp.float32), state, precision=lax.Precision.HIGHEST
    )
    total = cum[:, -1]
    scaled_keys = key_blk.astype(jnp.float32) * jnp.exp(total[:, None] - cum)[:, :, None]
    update = jnp.einsum(
        "hse,hsf->hef", scaled_keys, value_blk.astype(jnp.float32), precision=lax.Precision.HIGHEST
    )
    new_state = jnp.exp(total)[:, None, None] * state + update
    return (new_state, intra + inter)


def join_memory(earlier, later):
    return (earlier[0] + later[0], jnp.exp(later[0])[:, None, None] * earlier[1] + later[1])


def shards(queries, keys, values, log_decay, norm_gain, out_weight, steer_ids, steer_table):
    tok_rows, features = queries.shape
    heads_here = log_decay.shape[1]
    head_size = features // heads_here
    count = tok_rows // SPAN

    def split(array):
        return array.reshape(count, SPAN, heads_here, head_size).transpose(0, 2, 1, 3)

    decays = log_decay.reshape(count, SPAN, heads_here).transpose(0, 2, 1)
    start = jnp.zeros((heads_here, head_size, head_size), jnp.float32)
    local_memory, blocks = lax.scan(
        block_step, start, (split(queries), split(keys), split(values), decays)
    )
    device_log = jnp.sum(log_decay, axis=0)
    identity = (jnp.zeros((heads_here,), jnp.float32), start)
    passed = prefix((device_log, local_memory), "seq", join_memory, identity)
    earlier_memory = passed[1]
    running = jnp.cumsum(log_decay, axis=0)
    query_heads = queries.reshape(tok_rows, heads_here, head_size).astype(jnp.float32)
    carried = jnp.exp(running)[:, :, None] * jnp.einsum(
        "the,hef->thf", query_heads, earlier_memory, precision=lax.Precision.HIGHEST
    )
    attended = blocks.transpose(0, 2, 1, 3).reshape(tok_rows, heads_here, head_size) + carried
    mean_sq = jnp.mean(attended * attended, axis=-1, keepdims=True)
    normed = (attended * lax.rsqrt(mean_sq + 1e-06)).reshape(tok_rows, features) * norm_gain
    normed = normed.astype(jnp.bfloat16)
    partial_term = jnp.dot(normed, out_weight, preferred_element_type=jnp.float32)
    onehot = (
        steer_ids[:, None] == jnp.arange(steer_table.shape[0], dtype=jnp.int32)[None, :]
    ).astype(jnp.bfloat16)
    steering = jnp.dot(onehot, steer_table, preferred_element_type=jnp.float32)
    whole_sum = lax.psum(partial_term, "head")
    column_width = steer_table.shape[1]
    summed = lax.dynamic_slice_in_dim(
        whole_sum, lax.axis_index("head") * column_width, column_width, 1
    )
    return (summed + steering).astype(jnp.bfloat16)


def solution(mesh):
    in_specs = (
        P("seq", "head"),
        P("seq", "head"),
        P("seq", "head"),
        P("seq", "head"),
        P("head"),
        P("head", None),
        P("seq"),
        P(None, "head"),
    )
    out_specs = P("seq", "head")
    return jax.shard_map(shards, mesh=mesh, in_specs=in_specs, out_specs=out_specs, check_vma=False)
```

profile of v0, /device:TPU:2, one launch (start us, length us, event | category | flops | bytes accessed | tf_op | source)
XLA Modules:
  0.0 363.3 jit_solution(9025703200872860775)
XLA Ops:
  6.5 0.0 copy-start
  6.5 0.0 all-gather.4.cloned.1.call-start
  6.5 1.0 reduce_window_sum.23
  7.6 0.2 slice_reduce_fusion
  7.7 0.1 subtract_exponential_fusion
  7.8 1.0 copy.41
  8.9 0.9 reshape.85
  9.8 1.0 convolution_add_fusion
  10.8 0.0 all-gather.4.cloned.1.call-update
  10.8 0.0 all-reduce.3.cloned.1.call-start
  10.9 0.8 reduce_sum.18
  11.7 0.8 copy.33
  12.4 0.9 reshape.83
  13.4 1.3 dynamic-slice.5
  15.4 0.2 dynamic-update-slice
  15.6 129.7 %all-reduce = f32[256]{0:T(256)S(1)} all-reduce(f32[256]{0:T(256)S(1)} %dynamic-update-slice), channel_id=2, replica_groups=mesh['seq'=64,'head'=8] {'seq'}, use_global_device_ids=true, to_apply=%add | all-reduce | flops 256 | bytes 2048
  145.3 0.1 reshape.89
  145.5 0.2 reduce_window_sum.24
  145.7 0.1 copy.34
  145.8 0.4 fusion.7
  146.1 0.4 fusion.4
  146.5 61.4 %all-gather.4.cloned.1.call-done = f32[256,128,128]{2,1,0:T(8,128)} async-done(((f32[4,128,128]{2,1,0:T(8,128)}), f32[256,128,128]{2,1,0:T(8,128)}) %all-gather.4.cloned.1.call-update) | async-done | bytes 16777232 | tf_op jit(solution)/shard_map/all_gather | solution.py:11
  207.9 17.7 %while.3 = (s32[]{:T(128)}, f32[4,128,128]{2,1,0:T(8,128)S(1)}, s32[]{:T(128)}, f32[64,4]{1,0:T(8,128)S(1)}, f32[64,4,128,128]{3,2,1,0:T(8,128)}, /*index=5*/s32[]{:T(128)}, s32[]{:T(128)}, s32[]{:T(128)}) while((s32[]{:T(128)}, f32[4,128,128]{2,1,0:T(8,128)S(1)}, s32[]{:T(128)}, f32[64,4]{1,0:T(8,128)S(1)}, f32[64,4,128,128]{3,2,1,0:T(8,128)}, ...), condition=%wide.region_4.5_spmd, body=%wide.region_3.4_spmd.sunk | while | flops 131077 | bytes 786615 | solution.py:19
  207.9 1.1 bitcast_add_fusion.2
  209.0 1.1 bitcast_add_fusion.2
  210.1 1.1 bitcast_add_fusion.2
  211.2 1.1 bitcast_add_fusion.2
  212.4 1.1 bitcast_add_fusion.2
  213.5 1.1 bitcast_add_fusion.2
  214.6 1.1 bitcast_add_fusion.2
  215.7 1.1 bitcast_add_fusion.2
  216.8 1.1 bitcast_add_fusion.2
  217.9 1.1 bitcast_add_fusion.2
  219.0 1.1 bitcast_add_fusion.2
  220.1 1.1 bitcast_add_fusion.2
  221.2 1.1 bitcast_add_fusion.2
  222.3 1.1 bitcast_add_fusion.2
  223.4 1.1 bitcast_add_fusion.2
  224.5 1.1 bitcast_add_fusion.2
  225.6 0.0 copy-done.1
  225.6 0.4 multiply_reduce_fusion
  226.0 0.0 copy-done.2
  226.0 0.1 fusion.8
  226.2 0.0 copy-start.3
  226.2 4.2 %fusion.36 = f32[128,4096]{1,0:T(8,128)} fusion(bf16[128,512]{0,1:T(8,128)(2,1)S(1)} %fusion.8, bf16[512,4096]{1,0:T(8,128)(2,1)} %param.15), kind=kOutput, calls=%fused_computation.50 | convolution fusion | flops 536870912 | bytes 6422528 | tf_op jit(solution)/shard_map/dot_general | solution.py:76
  230.4 0.0 all-reduce.3.cloned.1.call-update
  230.5 124.1 %all-reduce.3.cloned.1.call-done = f32[128,4096]{1,0:T(8,128)} async-done(((f32[128,4096]{1,0:T(8,128)}), f32[128,4096]{1,0:T(8,128)}) %all-reduce.3.cloned.1.call-update) | async-done | bytes 2097168 | tf_op jit(solution)/shard_map/psum | solution.py:81
  354.6 1.8 fusion.6
  (27 shorter events, 0.3 us)
Async XLA Ops:
  6.5 348.1 %copy-start = (bf16[16,512]{1,0:T(8,128)(2,1)S(1)}, bf16[16,512]{1,0:T(8,128)(2,1)}, u32[]{:S(2)}) copy-start(bf16[16,512]{1,0:T(8,128)(2,1)} %param.17) | copy-start | bytes 49156
  6.5 219.0 %copy-start.1 = (bf16[128,512]{1,0:T(8,128)(2,1)S(1)}, bf16[128,512]{1,0:T(8,128)(2,1)}, u32[]{:S(2)}) copy-start(bf16[128,512]{1,0:T(8,128)(2,1)} %param.10) | copy-start | bytes 393220
  6.5 201.3 %all-gather.4.cloned.1.call-start = ((), (), s32[]{:S(2)}) async-start(), calls=%async_computation.1 | async-start | bytes 17039360 | tf_op jit(solution)/shard_map/all_gather | solution.py:11
  10.8 215.3 %copy-start.2 = (f32[512]{0:T(512)S(1)}, f32[512]{0:T(512)}, u32[]{:S(2)}) copy-start(f32[512]{0:T(512)} %param.14) | copy-start | bytes 6148
  10.8 343.8 %all-reduce.3.cloned.1.call-start = ((), (), s32[]{:S(2)}) async-start(), calls=%async_computation | async-start | bytes 4194304 | tf_op jit(solution)/shard_map/psum | solution.py:81
  226.2 128.4 %copy-start.3 = (s32[128]{0:T(128)S(1)}, s32[128]{0:T(128)}, u32[]{:S(2)}) copy-start(s32[128]{0:T(128)} %param.16) | copy-start | bytes 1540
Sparse Core Ops, SparseCore 0:
  10.9 196.8 all-gather.3
  230.6 123.9 all-reduce.2
where the time goes:
time: 366 us; the launch traced here: 363 us
  waiting for transfers between devices  186 us (51%)
  blocking collectives  130 us (36%)
  other arithmetic  19.2 us (5%)
  between operations  14.2 us (4%)
  matrix products  8.18 us (2%)
  local copies, waits for them, and re-layouts  5.91 us (2%)
    unnamed x1, blocking collectives  130 us
    psum x1, waiting for transfers between devices, shards(): whole_sum = lax.psum(partial_term, 'head')  124 us
    all_gather x1, waiting for transfers between devices, prefix(): gathered = jax.tree.map(lambda a: lax.all_gather(a, axis), part)  61.4 us
    add x16, other arithmetic, join_memory(): jnp.exp(later[0])[:, None, None] * earlier[1] + later[1]  17 us
  transfers between devices with their start and end apart: 2, of which 2 were waited for; matrix products, arithmetic and copies ran while one was open for 1% of the time, Pallas kernels for 0%

commit v1 on v0

--- a/solution.py
+++ b/solution.py
@@ -78,7 +78,13 @@
         steer_ids[:, None] == jnp.arange(steer_table.shape[0], dtype=jnp.int32)[None, :]
     ).astype(jnp.bfloat16)
     steering = jnp.dot(onehot, steer_table, preferred_element_type=jnp.float32)
-    whole_sum = lax.psum(partial_term, "head")
+    devices = lax.axis_size("head")
+    whole_sum, far = (partial_term, 1)
+    while far < devices:
+        whole_sum = whole_sum + lax.ppermute(
+            whole_sum, "head", [(i, i ^ far) for i in range(devices)]
+        )
+        far = 2 * far
     column_width = steer_table.shape[1]
     summed = lax.dynamic_slice_in_dim(
         whole_sum, lax.axis_index("head") * column_width, column_width, 1

time: 366 us -> 390 us (1.066)
  the two profiles are of different devices: /device:TPU:2 before, /device:TPU:486 now
where the time goes in v1:
time: 390 us; the launch traced here: 387 us
  waiting for transfers between devices  139 us (36%)
  blocking collectives  139 us (36%)
  other arithmetic  69.6 us (18%)
  between operations  14.2 us (4%)
  starting transfers between devices  10.2 us (3%)
  matrix products  6.88 us (2%)
  local copies, waits for them, and re-layouts  6.45 us (2%)
    unnamed x1, blocking collectives  139 us
    ppermute x3, waiting for transfers between devices, shards(): lax.ppermute(whole_sum, 'head', [(i, i ^ far) for i in range(devices)])  95.7 us
    add x63, other arithmetic, join_memory(): jnp.exp(later[0])[:, None, None] * earlier[1] + later[1]  66.9 us
    all_gather x1, waiting for transfers between devices, prefix(): gathered = jax.tree.map(lambda a: lax.all_gather(a, axis), part)  43.1 us
    ppermute x3, starting transfers between devices, shards(): lax.ppermute(whole_sum, 'head', [(i, i ^ far) for i in range(devices)])  10.2 us
  transfers between devices with their start and end apart: 4, of which 4 were waited for; matrix products, arithmetic and copies ran while one was open for 1% of the time, Pallas kernels for 0%

profile of v1, /device:TPU:486, one launch (start us, length us, event | category | flops | bytes accessed | tf_op | source)
XLA Modules:
  0.0 387.3 jit_solution(2469084908864610987)
XLA Ops:
  13.3 1.3 dynamic-slice.5
  15.5 139.3 %all-reduce = f32[256]{0:T(256)S(1)} all-reduce(f32[256]{0:T(256)S(1)} %dynamic-update-slice), channel_id=2, replica_groups=mesh['seq'=64,'head'=8] {'seq'}, use_global_device_ids=true, to_apply=%add | all-reduce | flops 256 | bytes 2048
  156.0 43.1 %all-gather.4.cloned.1.call-done = f32[256,128,128]{2,1,0:T(8,128)} async-done(((f32[4,128,128]{2,1,0:T(8,128)}), f32[256,128,128]{2,1,0:T(8,128)}) %all-gather.4.cloned.1.call-update) | async-done | bytes 16777232 | tf_op jit(solution)/shard_map/all_gather | solution.py:11
  199.1 69.5 %while.3 = (s32[]{:T(128)}, f32[4,128,128]{2,1,0:T(8,128)S(1)}, s32[]{:T(128)}, f32[64,4]{1,0:T(8,128)S(1)}, f32[64,4,128,128]{3,2,1,0:T(8,128)}, /*index=5*/s32[]{:T(128)}, s32[]{:T(128)}, s32[]{:T(128)}) while((s32[]{:T(128)}, f32[4,128,128]{2,1,0:T(8,128)S(1)}, s32[]{:T(128)}, f32[64,4]{1,0:T(8,128)S(1)}, f32[64,4,128,128]{3,2,1,0:T(8,128)}, ...), condition=%wide.region_4.5_spmd, body=%wide.region_3.4_spmd.sunk | while | flops 131077 | bytes 786615 | solution.py:19
  199.2 1.1 bitcast_add_fusion.2
  200.3 1.1 bitcast_add_fusion.2
  201.4 1.1 bitcast_add_fusion.2
  202.5 1.1 bitcast_add_fusion.2
  203.6 1.1 bitcast_add_fusion.2
  204.7 1.1 bitcast_add_fusion.2
  205.8 1.1 bitcast_add_fusion.2
  206.9 1.1 bitcast_add_fusion.2
  208.0 1.1 bitcast_add_fusion.2
  209.1 1.1 bitcast_add_fusion.2
  210.2 1.1 bitcast_add_fusion.2
  211.3 1.1 bitcast_add_fusion.2
  212.4 1.1 bitcast_add_fusion.2
  213.5 1.1 bitcast_add_fusion.2
  214.6 1.1 bitcast_add_fusion.2
  215.7 1.1 bitcast_add_fusion.2
  216.8 1.1 bitcast_add_fusion.2
  217.9 1.1 bitcast_add_fusion.2
  219.0 1.1 bitcast_add_fusion.2
  221.2 1.1 bitcast_add_fusion.2
  222.3 1.1 bitcast_add_fusion.2
  223.5 1.1 bitcast_add_fusion.2
  224.6 1.1 bitcast_add_fusion.2
  225.7 1.1 bitcast_add_fusion.2
  226.8 1.1 bitcast_add_fusion.2
  227.9 1.1 bitcast_add_fusion.2
  229.0 1.1 bitcast_add_fusion.2
  230.1 1.1 bitcast_add_fusion.2
  231.2 1.1 bitcast_add_fusion.2
  232.3 1.1 bitcast_add_fusion.2
  233.4 1.1 bitcast_add_fusion.2
  234.5 1.1 bitcast_add_fusion.2
  235.6 1.1 bitcast_add_fusion.2
  236.7 1.1 bitcast_add_fusion.2
  237.8 1.1 bitcast_add_fusion.2
  238.9 1.1 bitcast_add_fusion.2
  269.3 2.9 fusion.38
  272.2 1.9 collective-permute-start
  274.1 4.1 %collective-permute-done = f32[128,4096]{1,0:T(8,128)S(1)} collective-permute-done((f32[128,4096]{1,0:T(8,128)S(1)}, f32[128,4096]{1,0:T(8,128)S(1)}, u32[]{:S(2)}, u32[]{:S(2)}) %collective-permute-start) | collective-permute-done | bytes 2097184 | tf_op jit(solution)/shard_map/ppermute | solution.py:84
  278.5 3.4 collective-permute-start.1
  281.9 46.2 %collective-permute-done.1 = f32[128,4096]{1,0:T(8,128)S(1)} collective-permute-done((f32[128,4096]{1,0:T(8,128)S(1)}, f32[128,4096]{1,0:T(8,128)S(1)}, u32[]{:S(2)}, u32[]{:S(2)}) %collective-permute-start.1) | collective-permute-done | bytes 2097184 | tf_op jit(solution)/shard_map/ppermute | solution.py:84
  328.3 4.9 %collective-permute-start.2 = (f32[128,4096]{1,0:T(8,128)S(1)}, f32[128,4096]{1,0:T(8,128)}, u32[]{:S(2)}, u32[]{:S(2)}) collective-permute-start(f32[128,4096]{1,0:T(8,128)S(1)} %add.61), channel_id=1, source_target_pairs={{0,4},{1,5},{2,6},{3,7},{4,0},{5,1},{6,2},{7,3},{8,12},{9,13},{10,... | collective-permute-start | bytes 6291464 | tf_op jit(solution)/shard_map/ppermute | solution.py:84
  333.3 45.4 %collective-permute-done.2 = f32[128,4096]{1,0:T(8,128)} collective-permute-done((f32[128,4096]{1,0:T(8,128)S(1)}, f32[128,4096]{1,0:T(8,128)}, u32[]{:S(2)}, u32[]{:S(2)}) %collective-permute-start.2) | collective-permute-done | bytes 2097184 | tf_op jit(solution)/shard_map/ppermute | solution.py:84
  378.7 1.8 fusion.8
  (126 shorter events, 38.6 us)
Async XLA Ops:
  6.5 372.1 %copy-start = (bf16[16,512]{1,0:T(8,128)(2,1)S(1)}, bf16[16,512]{1,0:T(8,128)(2,1)}, u32[]{:S(2)}) copy-start(bf16[16,512]{1,0:T(8,128)(2,1)} %param.17) | copy-start | bytes 49156
  6.5 192.5 %all-gather.4.cloned.1.call-start = ((), (), s32[]{:S(2)}) async-start(), calls=%async_computation | async-start | bytes 17039360 | tf_op jit(solution)/shard_map/all_gather | solution.py:11
  199.1 69.5 %copy-start.1 = (bf16[128,512]{1,0:T(8,128)(2,1)S(1)}, bf16[128,512]{1,0:T(8,128)(2,1)}, u32[]{:S(2)}) copy-start(bf16[128,512]{1,0:T(8,128)(2,1)} %param.10) | copy-start | bytes 393220
  199.1 70.0 %copy-start.2 = (f32[512]{0:T(512)S(1)}, f32[512]{0:T(512)}, u32[]{:S(2)}) copy-start(f32[512]{0:T(512)} %param.14) | copy-start | bytes 6148
  272.2 6.1 %collective-permute-start = (f32[128,4096]{1,0:T(8,128)S(1)}, f32[128,4096]{1,0:T(8,128)S(1)}, u32[]{:S(2)}, u32[]{:S(2)}) collective-permute-start(f32[128,4096]{1,0:T(8,128)S(1)} %fusion.38), channel_id=1, source_target_pairs={{0,1},{1,0},{2,3},{3,2},{4,5},{5,4},{6,7},{7,6},{8,9},{9,8},{10,11... | collective-permute-start | bytes 6291464 | tf_op jit(solution)/shard_map/ppermute | solution.py:84
  278.5 100.1 %copy-start.3 = (s32[128]{0:T(128)S(1)}, s32[128]{0:T(128)}, u32[]{:S(2)}) copy-start(s32[128]{0:T(128)} %param.16) | copy-start | bytes 1540
  278.5 49.6 %collective-permute-start.1 = (f32[128,4096]{1,0:T(8,128)S(1)}, f32[128,4096]{1,0:T(8,128)S(1)}, u32[]{:S(2)}, u32[]{:S(2)}) collective-permute-start(f32[128,4096]{1,0:T(8,128)S(1)} %add.60), channel_id=1, source_target_pairs={{0,2},{1,3},{2,0},{3,1},{4,6},{5,7},{6,4},{7,5},{8,10},{9,11},{10,... | collective-permute-start | bytes 6291464 | tf_op jit(solution)/shard_map/ppermute | solution.py:84
  328.3 50.3 %collective-permute-start.2 = (f32[128,4096]{1,0:T(8,128)S(1)}, f32[128,4096]{1,0:T(8,128)}, u32[]{:S(2)}, u32[]{:S(2)}) collective-permute-start(f32[128,4096]{1,0:T(8,128)S(1)} %add.61), channel_id=1, source_target_pairs={{0,4},{1,5},{2,6},{3,7},{4,0},{5,1},{6,2},{7,3},{8,12},{9,13},{10,... | collective-permute-start | bytes 6291464 | tf_op jit(solution)/shard_map/ppermute | solution.py:84
Sparse Core Ops, SparseCore 0:
  10.9 188.1 all-gather.3
